TPU v7x, 512 devices: a whole 4x8x8 slice. The times are simulated.
512 devices in a mesh: rows: 32 (over y, x), vocab: 16 (over z, core).
Axes of the slice: x: 4, y: 8, z: 8, core: 2. Of those that a mesh axis runs over, the one named last changes fastest.
Arguments:
- hidden: bfloat16 [12288, 8192], P('rows', 'vocab'), may hold values from -128 to 128
- head: bfloat16 [8192, 8192], P('rows', 'vocab'), may hold values from -4 to 4
- targets: int32 [12288], P('rows'), may hold values from 0 to 128255
- live: int32 [12288], P('rows'), may hold values from 0 to 1, as said below
- prior_lse: float32 [12288], P('rows'), may hold values from 10 to 18
- prior_mean: float32 [12288], P('rows'), may hold values from 2 to 8
- prior_target: float32 [12288], P('rows'), may hold values from -12 to 12
- seq_lengths: int32 [32], replicated, may hold values from 1 to 768, 12288 in all
Outputs:
- logprob: float32 [12288], P(('rows', 'vocab'))
- entropy: float32 [12288], P(('rows', 'vocab'))
- seq_score: float32 [32], replicated
Inputs may be any that keep to these rules, and one draw needn't show every extreme that they name: Within the 384 rows of each index of rows, the live rows come first; every such index has at least 48 live rows and some index has all 384.
All inputs are finite; a program needn't handle non-finite values.
Results may differ from a plain program's by a relative error of at most 0.0003.
Values may be sent and summed in bfloat16 or wider, within the bound.
No kernel may reach another device: no remote copies, remote signals or barrier semaphores. Data moves between devices by JAX's collectives and lax.ppermute only.
A program may use at most 64 MiB of HBM per device.

v0:
```python
import jax
import jax.numpy as jnp
from jax import lax
from jax.sharding import PartitionSpec as P

VOCAB = 128256
SEQS = 32
GSIZE = 8


def finish_rows(block_peak, block_mass, block_moment, block_target, live, prior_lse, prior_mean):
    highest = jnp.maximum(block_peak, prior_lse)
    earlier = jnp.exp(prior_lse - highest)
    scaled = jnp.exp(block_peak - highest)
    total_mass = earlier + block_mass * scaled
    norm_log = highest + jnp.log(total_mass)
    average = (earlier * prior_mean + scaled * block_moment) / total_mass
    keeping = live.astype(jnp.float32)
    return (keeping * (block_target - norm_log), keeping * (norm_log - average))


def local(hidden, head, targets, live, prior_lse, prior_mean, prior_target, seq_lengths):
    rows_here = hidden.shape[0]
    cols_here = head.shape[1]
    spread = lax.axis_size("vocab")
    which = lax.axis_index("vocab")
    block_first = VOCAB - cols_here * spread
    first_col = block_first + which * cols_here
    gathered = lax.all_gather(hidden, "vocab", axis=1, tiled=True)
    logits = jnp.dot(
        gathered,
        lax.all_gather(head, "rows", axis=0, tiled=True),
        preferred_element_type=jnp.float32,
    )
    row_peak = jnp.max(logits, axis=1)
    weights = jnp.exp(logits - row_peak[:, None])
    row_mass = jnp.sum(weights, axis=1)
    moment = jnp.sum(weights * logits, axis=1)
    column = targets - first_col
    columns = lax.broadcasted_iota(jnp.int32, logits.shape, 1)
    picked = jnp.sum(jnp.where(columns == column[:, None], logits, jnp.zeros_like(logits)), axis=1)
    stats = jnp.stack([row_peak, row_mass, moment, picked])
    every = lax.all_gather(stats, "vocab", axis=0, tiled=False)
    peaks = every[:, 0]
    highest = jnp.max(peaks, axis=0)
    factor = jnp.exp(peaks - highest[None, :])
    mass_all = jnp.sum(every[:, 1] * factor, axis=0)
    moment_all = jnp.sum(every[:, 2] * factor, axis=0)
    picked_all = jnp.sum(every[:, 3], axis=0)
    block_target = jnp.where(targets >= block_first, picked_all, prior_target)
    logprob, entropy = finish_rows(
        highest, mass_all, moment_all, block_target, live, prior_lse, prior_mean
    )
    share = rows_here // spread
    begin = which * share
    logprob_share = lax.dynamic_slice_in_dim(logprob, begin, share, 0)
    entropy_share = lax.dynamic_slice_in_dim(entropy, begin, share, 0)
    global_rows = lax.axis_index("rows") * rows_here + jnp.arange(rows_here, dtype=jnp.int32)
    endings = jnp.cumsum(seq_lengths)
    member = jnp.sum((global_rows[:, None] >= endings[None, :]).astype(jnp.int32), axis=1)
    onehot = (member[:, None] == jnp.arange(SEQS, dtype=jnp.int32)[None, :]).astype(jnp.float32)
    partial_sums = jnp.sum(onehot * logprob[:, None], axis=0)
    sums = jnp.sum(lax.all_gather(partial_sums, "rows", axis=0, tiled=False), axis=0)
    seq_mean = sums / seq_lengths.astype(jnp.float32)
    grouped = seq_mean.reshape(SEQS // GSIZE, GSIZE)
    seq_score = (grouped - jnp.mean(grouped, axis=1, keepdims=True)).reshape(SEQS)
    return (logprob_share, entropy_share, seq_score)


def solution(mesh):
    return jax.shard_map(
        local,
        mesh=mesh,
        in_specs=(
            P("rows", "vocab"),
            P("rows", "vocab"),
            P("rows"),
            P("rows"),
            P("rows"),
            P("rows"),
            P("rows"),
            P(),
        ),
        out_specs=(P(("rows", "vocab")), P(("rows", "vocab")), P()),
        check_vma=False,
    )
```

profile of v0, /device:TPU:2, one launch (start us, length us, event | category | flops | bytes accessed | tf_op | source)
XLA Modules:
  0.0 275.6 jit_solution(6936003982868174059)
XLA Ops:
  7.2 0.0 all-gather.6.cloned.1.call-start
  7.2 0.7 all-gather.6.cloned.1.call-update
  7.9 0.0 all-gather.8.cloned.1.call-start
  7.9 0.7 all-gather.8.cloned.1.call-update
  8.7 0.7 copy.22
  9.4 0.1 reduce-window.8
  9.5 0.1 reduce.2
  9.6 1.3 dynamic-slice
  11.5 0.1 convert_reduce_fusion
  11.6 0.7 broadcast_subtract_fusion
  12.3 0.0 copy-start.4
  12.3 0.0 copy-start.5
  12.3 52.0 %all-gather.6.cloned.1.call-done = bf16[384,8192]{1,0:T(8,128)(2,1)} async-done(((bf16[384,512]{1,0:T(8,128)(2,1)}), bf16[384,8192]{1,0:T(8,128)(2,1)}) %all-gather.6.cloned.1.call-update) | async-done | bytes 6291472 | tf_op jit(solution)/shard_map/all_gather | solution.py:29
  64.3 103.5 %all-gather.8.cloned.1.call-done = bf16[8192,512]{1,0:T(8,128)(2,1)} async-done(((bf16[256,512]{1,0:T(8,128)(2,1)}), bf16[8192,512]{1,0:T(8,128)(2,1)}) %all-gather.8.cloned.1.call-update) | async-done | bytes 8388624 | tf_op jit(solution)/shard_map/all_gather | solution.py:32
  167.7 8.0 %fusion.7 = (f32[384]{0:T(512)S(1)}, f32[384,512]{1,0:T(8,128)S(1)}) fusion(bf16[384,8192]{1,0:T(8,128)(2,1)} %all-gather.6.cloned.1.call-done, bf16[8192,512]{1,0:T(8,128)(2,1)} %all-gather.8.cloned.1.call-done), kind=kOutput, calls=%fused_computation.30 | convolution fusion | flops 3221421568 | bytes 15468032 | tf_op jit(solution)/shard_map/dot_general | solution.py:30
  175.8 0.5 fusion
  176.3 18.3 %all-gather.2 = f32[16,4,384]{2,1,0:T(4,128)S(1)} all-gather(f32[1,4,384]{2,1,0:T(4,128)S(1)} %maximum_bitcast_fusion), channel_id=2, replica_groups=mesh['rows'=32,'vocab'=16] {'vocab'}, dimensions={0}, use_global_device_ids=true | all-gather | bytes 104448 | tf_op jit(solution)/shard_map/all_gather | solution.py:43
  194.6 0.1 fusion.6
  194.8 0.0 copy-done
  194.8 0.0 copy-done.1
  194.8 0.6 dynamic_slice.6
  195.4 0.6 dynamic_slice.7
  196.0 0.1 select_reduce_fusion.1
  196.1 0.2 dynamic-update-slice
  196.4 71.4 %all-reduce = f32[1024]{0:T(1024)S(1)} all-reduce(f32[1024]{0:T(1024)S(1)} %dynamic-update-slice), channel_id=3, replica_groups=mesh['rows'=32,'vocab'=16] {'rows'}, use_global_device_ids=true, to_apply=%add | all-reduce | flops 1024 | bytes 8192
  267.8 0.1 reshape.52
  267.9 0.0 copy-done.5
  267.9 0.1 reshape.50
  268.0 0.1 reduce_sum.99
  268.1 0.1 sub.55
  268.2 0.1 sub.56
  268.2 0.5 sub.57
  (19 shorter events, 0.1 us)
Async XLA Ops:
  7.2 57.1 %all-gather.6.cloned.1.call-start = ((), (), s32[]{:S(2)}) async-start(), calls=%async_computation | async-start | bytes 6684672 | tf_op jit(solution)/shard_map/all_gather | solution.py:29
  7.9 159.8 %all-gather.8.cloned.1.call-start = ((), (), s32[]{:S(2)}) async-start(), calls=%async_computation.1 | async-start | bytes 8650752 | tf_op jit(solution)/shard_map/all_gather | solution.py:32
  12.3 182.5 %copy-start = (s32[384]{0:T(512)S(1)}, s32[384]{0:T(512)}, u32[]{:S(2)}) copy-start(s32[384]{0:T(512)} %param.10) | copy-start | bytes 4612
  12.3 182.5 %copy-start.1 = (f32[384]{0:T(512)S(1)}, f32[384]{0:T(512)}, u32[]{:S(2)}) copy-start(f32[384]{0:T(512)} %param.13) | copy-start | bytes 4612
  12.3 182.5 %copy-start.2 = (s32[384]{0:T(512)S(1)}, s32[384]{0:T(512)}, u32[]{:S(2)}) copy-start(s32[384]{0:T(512)} %param.11) | copy-start | bytes 4612
  12.3 182.5 %copy-start.3 = (f32[384]{0:T(512)S(1)}, f32[384]{0:T(512)}, u32[]{:S(2)}) copy-start(f32[384]{0:T(512)} %param.12) | copy-start | bytes 4612
  12.3 182.5 %copy-start.4 = (f32[384]{0:T(512)S(1)}, f32[384]{0:T(512)}, u32[]{:S(2)}) copy-start(f32[384]{0:T(512)} %param.14) | copy-start | bytes 4612
  12.3 255.5 %copy-start.5 = (s32[32]{0:T(128)S(1)}, s32[32]{0:T(128)}, u32[]{:S(2)}) copy-start(s32[32]{0:T(128)} %param.15) | copy-start | bytes 388
Sparse Core Ops, SparseCore 0:
  10.1 54.0 all-gather.5
  67.4 100.2 all-gather.7
where the time goes:
time: 276 us
  waiting for transfers between devices  157 us (57%)
  blocking collectives  89.7 us (32%)
  between operations  14.8 us (5%)
  matrix products  8 us (3%)
  local copies, waits for them, and re-layouts  3.78 us (1%)
    all_gather x1, waiting for transfers between devices, local(): lax.all_gather(head, 'rows', axis=0, tiled=True)  103 us
    unnamed x1, blocking collectives  71.4 us
    all_gather x1, waiting for transfers between devices, local(): gathered = lax.all_gather(hidden, 'vocab', axis=1, tiled=True)  52 us
    all_gather x1, blocking collectives, local(): every = lax.all_gather(stats, 'vocab', axis=0, tiled=False)  18.3 us
    dot_general x1, matrix products, local(): jnp.dot(gathered, lax.all_gather(head, 'rows', axis=0, tiled=True), prefe...  8 us
  transfers between devices with their start and end apart: 2, of which 2 were waited for; matrix products, arithmetic and copies ran while one was open for 1% of the time, Pallas kernels for 0%

commit v1 on v0

--- a/solution.py
+++ b/solution.py
@@ -6,6 +6,12 @@
 VOCAB = 128256
 SEQS = 32
 GSIZE = 8
+
+
+def laid_out(tiles, dim):
+    tiles = jnp.moveaxis(tiles, 0, dim)
+    shape = tiles.shape
+    return tiles.reshape(*shape[:dim], shape[dim] * shape[dim + 1], *shape[dim + 2 :])
 
 
 def finish_rows(block_peak, block_mass, block_moment, block_target, live, prior_lse, prior_mean):
@@ -26,7 +32,19 @@
     which = lax.axis_index("vocab")
     block_first = VOCAB - cols_here * spread
     first_col = block_first + which * cols_here
-    gathered = lax.all_gather(hidden, "vocab", axis=1, tiled=True)
+    size = lax.axis_size("vocab")
+    pairs = [(i, (i + 1) % size) for i in range(size)]
+    back = [(b, a) for a, b in pairs]
+    lower, upper = ([], [])
+    for step in range(size - 1):
+        if step % 2 == 0:
+            lower.append(lax.ppermute(lower[-1] if lower else hidden, "vocab", pairs))
+        else:
+            upper.append(lax.ppermute(upper[-1] if upper else hidden, "vocab", back))
+    blocks = jnp.stack([*lower[::-1], hidden, *upper])
+    shift = lax.axis_index("vocab") - len(lower)
+    blocks = blocks[(jnp.arange(size) - shift) % size]
+    gathered = laid_out(blocks, 1)
     logits = jnp.dot(
         gathered,
         lax.all_gather(head, "rows", axis=0, tiled=True),

time: 276 us -> 227 us (0.82)
  waiting for transfers between devices: 157 us -> 48.5 us
  local copies, waits for them, and re-layouts: 3.78 us -> 37.8 us
  starting transfers between devices: 0.08 us -> 21.4 us
  other arithmetic: 2.39 us -> 5.54 us
    all_gather x1, waiting for transfers between devices: 103 us -> 2.08 us  [local(): lax.all_gather(head, 'rows', axis=0, tiled=True)]
    all_gather x1 -> x0, waiting for transfers between devices: 52 us -> none  [local(): gathered = lax.all_gather(hidden, 'vocab', axis=1, tiled=True)]
    ppermute x0 -> x15, waiting for transfers between devices: none -> 45.7 us  [the longest x8 45 us: local(): lower.append(lax.ppermute(lower[-1] if lower else hidden, 'vocab', pairs))]
    ppermute x0 -> x15, starting transfers between devices: none -> 21.4 us  [the longest x7 21.3 us: local(): upper.append(lax.ppermute(upper[-1] if upper else hidden, 'vocab', back))]
    unnamed x15 -> x34, local copies, waits for them, and re-layouts: 1.55 us -> 19.7 us
    transpose x0 -> x1, local copies, waits for them, and re-layouts: none -> 8.61 us  [laid_out(): tiles = jnp.moveaxis(tiles, 0, dim)]
    gather x0 -> x1, local copies, waits for them, and re-layouts: none -> 6.46 us  [local(): blocks = blocks[(jnp.arange(size) - shift) % size]]
  transfers between devices with their start and end apart: 2 -> 16, of which waited for: 2 -> 10; matrix products, arithmetic and copies ran while one was open for 1% -> 18% of each run, Pallas kernels for 0% -> 0%
where the time goes in v1:
time: 227 us; the launch traced here: 226 us
  blocking collectives  89.7 us (40%)
  waiting for transfers between devices  48.5 us (21%)
  local copies, waits for them, and re-layouts  37.8 us (17%)
  starting transfers between devices  21.4 us (9%)
  between operations  14.9 us (7%)
  matrix products  8.12 us (4%)
  other arithmetic  5.54 us (2%)
    unnamed x1, blocking collectives  71.4 us
    ppermute x8, waiting for transfers between devices, local(): lower.append(lax.ppermute(lower[-1] if lower else hidden, 'vocab', pairs))  45 us
    ppermute x7, starting transfers between devices, local(): upper.append(lax.ppermute(upper[-1] if upper else hidden, 'vocab', back))  21.3 us
    unnamed x34, local copies, waits for them, and re-layouts  19.7 us
    all_gather x1, blocking collectives, local(): every = lax.all_gather(stats, 'vocab', axis=0, tiled=False)  18.3 us
    transpose x1, local copies, waits for them, and re-layouts, laid_out(): tiles = jnp.moveaxis(tiles, 0, dim)  8.61 us
    dot_general x1, matrix products, local(): jnp.dot(gathered, lax.all_gather(head, 'rows', axis=0, tiled=True), prefe...  8.12 us
    gather x1, local copies, waits for them, and re-layouts, local(): blocks = blocks[(jnp.arange(size) - shift) % size]  6.46 us
  transfers between devices with their start and end apart: 16, of which 10 were waited for; matrix products, arithmetic and copies ran while one was open for 18% of the time, Pallas kernels for 0%

profile of v1, /device:TPU:2, one launch (start us, length us, event | category | flops | bytes accessed | tf_op | source)
XLA Modules:
  0.0 225.9 jit_solution(264909723769320608)
XLA Ops:
  7.9 14.1 %collective-permute-done = bf16[384,512]{1,0:T(8,128)(2,1)S(1)} collective-permute-done((bf16[384,512]{1,0:T(8,128)(2,1)}, bf16[384,512]{1,0:T(8,128)(2,1)S(1)}, u32[]{:S(2)}, u32[]{:S(2)}) %collective-permute-start) | collective-permute-done | bytes 393248 | tf_op jit(solution)/shard_map/ppermute | solution.py:41
  22.1 3.0 %collective-permute-start.8 = (bf16[384,512]{1,0:T(8,128)(2,1)}, bf16[384,512]{1,0:T(8,128)(2,1)S(1)}, u32[]{:S(2)}, u32[]{:S(2)}) collective-permute-start(bf16[384,512]{1,0:T(8,128)(2,1)} %param.8), channel_id=1, source_target_pairs={{1,0},{2,1},{3,2},{4,3},{5,4},{6,5},{7,6},{8,7},{9,8},{10,9},{11,1... | collective-permute-start | bytes 1179656 | tf_op jit(solution)/shard_map/ppermute | solution.py:43
  25.0 5.5 %collective-permute-done.1 = bf16[384,512]{1,0:T(8,128)(2,1)S(1)} collective-permute-done((bf16[384,512]{1,0:T(8,128)(2,1)S(1)}, bf16[384,512]{1,0:T(8,128)(2,1)S(1)}, u32[]{:S(2)}, u32[]{:S(2)}) %collective-permute-start.1) | collective-permute-done | bytes 393248 | tf_op jit(solution)/shard_map/ppermute | solution.py:41
  30.6 3.0 %collective-permute-start.9 = (bf16[384,512]{1,0:T(8,128)(2,1)S(1)}, bf16[384,512]{1,0:T(8,128)(2,1)S(1)}, u32[]{:S(2)}, u32[]{:S(2)}) collective-permute-start(bf16[384,512]{1,0:T(8,128)(2,1)S(1)} %collective-permute-done.8), channel_id=1, source_target_pairs={{1,0},{2,1},{3,2},{4,3},{5,4},{6,5},{7,6},{8,7},{9,8},{10,9},{11,1... | collective-permute-start | bytes 1179656 | tf_op jit(solution)/shard_map/ppermute | solution.py:43
  33.7 5.2 %collective-permute-done.2 = bf16[384,512]{1,0:T(8,128)(2,1)S(1)} collective-permute-done((bf16[384,512]{1,0:T(8,128)(2,1)S(1)}, bf16[384,512]{1,0:T(8,128)(2,1)S(1)}, u32[]{:S(2)}, u32[]{:S(2)}) %collective-permute-start.2) | collective-permute-done | bytes 393248 | tf_op jit(solution)/shard_map/ppermute | solution.py:41
  38.9 3.1 %collective-permute-start.10 = (bf16[384,512]{1,0:T(8,128)(2,1)S(1)}, bf16[384,512]{1,0:T(8,128)(2,1)S(1)}, u32[]{:S(2)}, u32[]{:S(2)}) collective-permute-start(bf16[384,512]{1,0:T(8,128)(2,1)S(1)} %collective-permute-done.9), channel_id=1, source_target_pairs={{1,0},{2,1},{3,2},{4,3},{5,4},{6,5},{7,6},{8,7},{9,8},{10,9},{11,1... | collective-permute-start | bytes 1179656 | tf_op jit(solution)/shard_map/ppermute | solution.py:43
  42.1 5.2 %collective-permute-done.3 = bf16[384,512]{1,0:T(8,128)(2,1)S(1)} collective-permute-done((bf16[384,512]{1,0:T(8,128)(2,1)S(1)}, bf16[384,512]{1,0:T(8,128)(2,1)S(1)}, u32[]{:S(2)}, u32[]{:S(2)}) %collective-permute-start.3) | collective-permute-done | bytes 393248 | tf_op jit(solution)/shard_map/ppermute | solution.py:41
  47.4 3.5 %collective-permute-start.11 = (bf16[384,512]{1,0:T(8,128)(2,1)S(1)}, bf16[384,512]{1,0:T(8,128)(2,1)S(1)}, u32[]{:S(2)}, u32[]{:S(2)}) collective-permute-start(bf16[384,512]{1,0:T(8,128)(2,1)S(1)} %collective-permute-done.10), channel_id=1, source_target_pairs={{1,0},{2,1},{3,2},{4,3},{5,4},{6,5},{7,6},{8,7},{9,8},{10,9},{11,1... | collective-permute-start | bytes 1179656 | tf_op jit(solution)/shard_map/ppermute | solution.py:43
  50.9 4.8 %collective-permute-done.4 = bf16[384,512]{1,0:T(8,128)(2,1)S(1)} collective-permute-done((bf16[384,512]{1,0:T(8,128)(2,1)S(1)}, bf16[384,512]{1,0:T(8,128)(2,1)S(1)}, u32[]{:S(2)}, u32[]{:S(2)}) %collective-permute-start.4) | collective-permute-done | bytes 393248 | tf_op jit(solution)/shard_map/ppermute | solution.py:41
  56.5 2.8 %collective-permute-start.12 = (bf16[384,512]{1,0:T(8,128)(2,1)S(1)}, bf16[384,512]{1,0:T(8,128)(2,1)}, u32[]{:S(2)}, u32[]{:S(2)}) collective-permute-start(bf16[384,512]{1,0:T(8,128)(2,1)S(1)} %collective-permute-done.11), channel_id=1, source_target_pairs={{1,0},{2,1},{3,2},{4,3},{5,4},{6,5},{7,6},{8,7},{9,8},{10,9},{11,1... | collective-permute-start | bytes 1179656 | tf_op jit(solution)/shard_map/ppermute | solution.py:43
  59.3 4.9 %collective-permute-done.5 = bf16[384,512]{1,0:T(8,128)(2,1)} collective-permute-done((bf16[384,512]{1,0:T(8,128)(2,1)S(1)}, bf16[384,512]{1,0:T(8,128)(2,1)}, u32[]{:S(2)}, u32[]{:S(2)}) %collective-permute-start.5) | collective-permute-done | bytes 393248 | tf_op jit(solution)/shard_map/ppermute | solution.py:41
  64.9 3.0 %collective-permute-start.13 = (bf16[384,512]{1,0:T(8,128)(2,1)}, bf16[384,512]{1,0:T(8,128)(2,1)}, u32[]{:S(2)}, u32[]{:S(2)}) collective-permute-start(bf16[384,512]{1,0:T(8,128)(2,1)} %collective-permute-done.12), channel_id=1, source_target_pairs={{1,0},{2,1},{3,2},{4,3},{5,4},{6,5},{7,6},{8,7},{9,8},{10,9},{11,1... | collective-permute-start | bytes 1179656 | tf_op jit(solution)/shard_map/ppermute | solution.py:43
  67.8 5.2 %collective-permute-done.6 = bf16[384,512]{1,0:T(8,128)(2,1)} collective-permute-done((bf16[384,512]{1,0:T(8,128)(2,1)}, bf16[384,512]{1,0:T(8,128)(2,1)}, u32[]{:S(2)}, u32[]{:S(2)}) %collective-permute-start.6) | collective-permute-done | bytes 393248 | tf_op jit(solution)/shard_map/ppermute | solution.py:41
  74.9 0.8 reduce.2
  75.8 1.3 dynamic-slice
  79.1 3.0 %collective-permute-start.14 = (bf16[384,512]{1,0:T(8,128)(2,1)}, bf16[384,512]{1,0:T(8,128)(2,1)S(1)}, u32[]{:S(2)}, u32[]{:S(2)}) collective-permute-start(bf16[384,512]{1,0:T(8,128)(2,1)} %collective-permute-done.13), channel_id=1, source_target_pairs={{1,0},{2,1},{3,2},{4,3},{5,4},{6,5},{7,6},{8,7},{9,8},{10,9},{11,1... | collective-permute-start | bytes 1179656 | tf_op jit(solution)/shard_map/ppermute | solution.py:43
  82.1 1.8 bitcast_dynamic-update-slice_fusion.15
  83.9 1.8 bitcast_dynamic-update-slice_fusion.14
  85.7 1.8 bitcast_dynamic-update-slice_fusion.13
  87.5 1.8 bitcast_dynamic-update-slice_fusion.12
  90.1 0.8 bitcast_dynamic-update-slice_fusion.10
  90.9 0.8 bitcast_dynamic-update-slice_fusion.9
  91.7 0.8 bitcast_dynamic-update-slice_fusion.8
  95.6 0.8 bitcast_dynamic-update-slice_fusion.3
  96.4 1.8 bitcast_dynamic-update-slice_fusion.2
  98.2 1.8 bitcast_dynamic-update-slice_fusion.1
  100.8 6.5 %gather_fusion = bf16[16,384,512]{2,1,0:T(8,128)(2,1)} fusion(bf16[16,384,512]{2,1,0:T(8,128)(2,1)} %bitcast_dynamic-update-slice_fusion, s32[1024]{0:T(1024)} %pad_clamp_fusion), kind=kCustom, calls=%fused_computation | custom fusion | bytes 12582976 | tf_op jit(solution)/shard_map/gather | solution.py:46
  107.2 8.6 %copy.25 = bf16[384,16,512]{0,2,1:T(8,128)(2,1)} copy(bf16[384,16,512]{2,0,1:T(8,128)(2,1)} %bitcast.63) | data formatting | bytes 12582912 | tf_op jit(solution)/shard_map/transpose | solution.py:12
  115.8 2.1 all-gather.5.cloned.1.call-done
  117.9 8.1 %fusion.9 = (f32[384]{0:T(512)S(1)}, f32[384,512]{1,0:T(8,128)S(1)}) fusion(bf16[384,8192]{0,1:T(8,128)(2,1)} %bitcast.62, bf16[8192,512]{1,0:T(8,128)(2,1)} %all-gather.5.cloned.1.call-done), kind=kOutput, calls=%fused_computation.54 | convolution fusion | flops 3221421568 | bytes 15468032 | tf_op jit(solution)/shard_map/dot_general | solution.py:48
  126.6 18.3 %all-gather.2 = f32[16,4,384]{2,1,0:T(4,128)S(1)} all-gather(f32[1,4,384]{2,1,0:T(4,128)S(1)} %maximum_bitcast_fusion), channel_id=2, replica_groups=mesh['rows'=32,'vocab'=16] {'vocab'}, dimensions={0}, use_global_device_ids=true | all-gather | bytes 104448 | tf_op jit(solution)/shard_map/all_gather | solution.py:61
  145.5 71.4 %all-reduce = f32[1024]{0:T(1024)S(1)} all-reduce(f32[1024]{0:T(1024)S(1)} %dynamic-update-slice), channel_id=3, replica_groups=mesh['rows'=32,'vocab'=16] {'rows'}, use_global_device_ids=true, to_apply=%add | all-reduce | flops 1024 | bytes 8192
  (70 shorter events, 13.7 us)
Async XLA Ops:
  7.2 85.3 %copy-start = (bf16[384,512]{1,0:T(8,128)(2,1)S(1)}, bf16[384,512]{1,0:T(8,128)(2,1)}, u32[]{:S(2)}) copy-start(bf16[384,512]{1,0:T(8,128)(2,1)} %param.8) | copy-start | bytes 1179652
  7.2 110.7 %all-gather.5.cloned.1.call-start = ((), (), s32[]{:S(2)}) async-start(), calls=%async_computation | async-start | bytes 8650752 | tf_op jit(solution)/shard_map/all_gather | solution.py:50
  7.9 14.2 %collective-permute-start = (bf16[384,512]{1,0:T(8,128)(2,1)}, bf16[384,512]{1,0:T(8,128)(2,1)S(1)}, u32[]{:S(2)}, u32[]{:S(2)}) collective-permute-start(bf16[384,512]{1,0:T(8,128)(2,1)} %param.8), channel_id=1, source_target_pairs={{0,1},{1,2},{2,3},{3,4},{4,5},{5,6},{6,7},{7,8},{8,9},{9,10},{10,1... | collective-permute-start | bytes 1179656 | tf_op jit(solution)/shard_map/ppermute | solution.py:41
  22.1 8.4 %collective-permute-start.1 = (bf16[384,512]{1,0:T(8,128)(2,1)S(1)}, bf16[384,512]{1,0:T(8,128)(2,1)S(1)}, u32[]{:S(2)}, u32[]{:S(2)}) collective-permute-start(bf16[384,512]{1,0:T(8,128)(2,1)S(1)} %collective-permute-done), channel_id=1, source_target_pairs={{0,1},{1,2},{2,3},{3,4},{4,5},{5,6},{6,7},{7,8},{8,9},{9,10},{10,1... | collective-permute-start | bytes 1179656 | tf_op jit(solution)/shard_map/ppermute | solution.py:41
  22.1 8.6 %collective-permute-start.8 = (bf16[384,512]{1,0:T(8,128)(2,1)}, bf16[384,512]{1,0:T(8,128)(2,1)S(1)}, u32[]{:S(2)}, u32[]{:S(2)}) collective-permute-start(bf16[384,512]{1,0:T(8,128)(2,1)} %param.8), channel_id=1, source_target_pairs={{1,0},{2,1},{3,2},{4,3},{5,4},{6,5},{7,6},{8,7},{9,8},{10,9},{11,1... | collective-permute-start | bytes 1179656 | tf_op jit(solution)/shard_map/ppermute | solution.py:43
  30.5 8.4 %collective-permute-start.2 = (bf16[384,512]{1,0:T(8,128)(2,1)S(1)}, bf16[384,512]{1,0:T(8,128)(2,1)S(1)}, u32[]{:S(2)}, u32[]{:S(2)}) collective-permute-start(bf16[384,512]{1,0:T(8,128)(2,1)S(1)} %collective-permute-done.1), channel_id=1, source_target_pairs={{0,1},{1,2},{2,3},{3,4},{4,5},{5,6},{6,7},{7,8},{8,9},{9,10},{10,1... | collective-permute-start | bytes 1179656 | tf_op jit(solution)/shard_map/ppermute | solution.py:41
  30.6 8.3 %collective-permute-start.9 = (bf16[384,512]{1,0:T(8,128)(2,1)S(1)}, bf16[384,512]{1,0:T(8,128)(2,1)S(1)}, u32[]{:S(2)}, u32[]{:S(2)}) collective-permute-start(bf16[384,512]{1,0:T(8,128)(2,1)S(1)} %collective-permute-done.8), channel_id=1, source_target_pairs={{1,0},{2,1},{3,2},{4,3},{5,4},{6,5},{7,6},{8,7},{9,8},{10,9},{11,1... | collective-permute-start | bytes 1179656 | tf_op jit(solution)/shard_map/ppermute | solution.py:43
  38.9 8.4 %collective-permute-start.3 = (bf16[384,512]{1,0:T(8,128)(2,1)S(1)}, bf16[384,512]{1,0:T(8,128)(2,1)S(1)}, u32[]{:S(2)}, u32[]{:S(2)}) collective-permute-start(bf16[384,512]{1,0:T(8,128)(2,1)S(1)} %collective-permute-done.2), channel_id=1, source_target_pairs={{0,1},{1,2},{2,3},{3,4},{4,5},{5,6},{6,7},{7,8},{8,9},{9,10},{10,1... | collective-permute-start | bytes 1179656 | tf_op jit(solution)/shard_map/ppermute | solution.py:41
  38.9 8.4 %collective-permute-start.10 = (bf16[384,512]{1,0:T(8,128)(2,1)S(1)}, bf16[384,512]{1,0:T(8,128)(2,1)S(1)}, u32[]{:S(2)}, u32[]{:S(2)}) collective-permute-start(bf16[384,512]{1,0:T(8,128)(2,1)S(1)} %collective-permute-done.9), channel_id=1, source_target_pairs={{1,0},{2,1},{3,2},{4,3},{5,4},{6,5},{7,6},{8,7},{9,8},{10,9},{11,1... | collective-permute-start | bytes 1179656 | tf_op jit(solution)/shard_map/ppermute | solution.py:43
  47.3 8.4 %collective-permute-start.4 = (bf16[384,512]{1,0:T(8,128)(2,1)S(1)}, bf16[384,512]{1,0:T(8,128)(2,1)S(1)}, u32[]{:S(2)}, u32[]{:S(2)}) collective-permute-start(bf16[384,512]{1,0:T(8,128)(2,1)S(1)} %collective-permute-done.3), channel_id=1, source_target_pairs={{0,1},{1,2},{2,3},{3,4},{4,5},{5,6},{6,7},{7,8},{8,9},{9,10},{10,1... | collective-permute-start | bytes 1179656 | tf_op jit(solution)/shard_map/ppermute | solution.py:41
  47.4 8.8 %collective-permute-start.11 = (bf16[384,512]{1,0:T(8,128)(2,1)S(1)}, bf16[384,512]{1,0:T(8,128)(2,1)S(1)}, u32[]{:S(2)}, u32[]{:S(2)}) collective-permute-start(bf16[384,512]{1,0:T(8,128)(2,1)S(1)} %collective-permute-done.10), channel_id=1, source_target_pairs={{1,0},{2,1},{3,2},{4,3},{5,4},{6,5},{7,6},{8,7},{9,8},{10,9},{11,1... | collective-permute-start | bytes 1179656 | tf_op jit(solution)/shard_map/ppermute | solution.py:43
  55.7 0.8 copy-start.1
  55.7 8.5 %collective-permute-start.5 = (bf16[384,512]{1,0:T(8,128)(2,1)S(1)}, bf16[384,512]{1,0:T(8,128)(2,1)}, u32[]{:S(2)}, u32[]{:S(2)}) collective-permute-start(bf16[384,512]{1,0:T(8,128)(2,1)S(1)} %collective-permute-done.4), channel_id=1, source_target_pairs={{0,1},{1,2},{2,3},{3,4},{4,5},{5,6},{6,7},{7,8},{8,9},{9,10},{10,1... | collective-permute-start | bytes 1179656 | tf_op jit(solution)/shard_map/ppermute | solution.py:41
  56.5 8.4 %collective-permute-start.12 = (bf16[384,512]{1,0:T(8,128)(2,1)S(1)}, bf16[384,512]{1,0:T(8,128)(2,1)}, u32[]{:S(2)}, u32[]{:S(2)}) collective-permute-start(bf16[384,512]{1,0:T(8,128)(2,1)S(1)} %collective-permute-done.11), channel_id=1, source_target_pairs={{1,0},{2,1},{3,2},{4,3},{5,4},{6,5},{7,6},{8,7},{9,8},{10,9},{11,1... | collective-permute-start | bytes 1179656 | tf_op jit(solution)/shard_map/ppermute | solution.py:43
  64.2 8.7 %collective-permute-start.6 = (bf16[384,512]{1,0:T(8,128)(2,1)}, bf16[384,512]{1,0:T(8,128)(2,1)}, u32[]{:S(2)}, u32[]{:S(2)}) collective-permute-start(bf16[384,512]{1,0:T(8,128)(2,1)} %collective-permute-done.5), channel_id=1, source_target_pairs={{0,1},{1,2},{2,3},{3,4},{4,5},{5,6},{6,7},{7,8},{8,9},{9,10},{10,1... | collective-permute-start | bytes 1179656 | tf_op jit(solution)/shard_map/ppermute | solution.py:41
  64.9 14.3 %collective-permute-start.13 = (bf16[384,512]{1,0:T(8,128)(2,1)}, bf16[384,512]{1,0:T(8,128)(2,1)}, u32[]{:S(2)}, u32[]{:S(2)}) collective-permute-start(bf16[384,512]{1,0:T(8,128)(2,1)} %collective-permute-done.12), channel_id=1, source_target_pairs={{1,0},{2,1},{3,2},{4,3},{5,4},{6,5},{7,6},{8,7},{9,8},{10,9},{11,1... | collective-permute-start | bytes 1179656 | tf_op jit(solution)/shard_map/ppermute | solution.py:43
  73.0 9.1 %collective-permute-start.7 = (bf16[384,512]{1,0:T(8,128)(2,1)}, bf16[384,512]{1,0:T(8,128)(2,1)}, u32[]{:S(2)}, u32[]{:S(2)}) collective-permute-start(bf16[384,512]{1,0:T(8,128)(2,1)} %collective-permute-done.6), channel_id=1, source_target_pairs={{0,1},{1,2},{2,3},{3,4},{4,5},{5,6},{6,7},{7,8},{8,9},{9,10},{10,1... | collective-permute-start | bytes 1179656 | tf_op jit(solution)/shard_map/ppermute | solution.py:41
  79.1 20.8 %collective-permute-start.14 = (bf16[384,512]{1,0:T(8,128)(2,1)}, bf16[384,512]{1,0:T(8,128)(2,1)S(1)}, u32[]{:S(2)}, u32[]{:S(2)}) collective-permute-start(bf16[384,512]{1,0:T(8,128)(2,1)} %collective-permute-done.13), channel_id=1, source_target_pairs={{1,0},{2,1},{3,2},{4,3},{5,4},{6,5},{7,6},{8,7},{9,8},{10,9},{11,1... | collective-permute-start | bytes 1179656 | tf_op jit(solution)/shard_map/ppermute | solution.py:43
  117.9 27.2 %copy-start.2 = (s32[384]{0:T(512)S(1)}, s32[384]{0:T(512)}, u32[]{:S(2)}) copy-start(s32[384]{0:T(512)} %param.10) | copy-start | bytes 4612
  117.9 27.2 %copy-start.3 = (f32[384]{0:T(512)S(1)}, f32[384]{0:T(512)}, u32[]{:S(2)}) copy-start(f32[384]{0:T(512)} %param.13) | copy-start | bytes 4612
  117.9 27.2 %copy-start.4 = (s32[384]{0:T(512)S(1)}, s32[384]{0:T(512)}, u32[]{:S(2)}) copy-start(s32[384]{0:T(512)} %param.11) | copy-start | bytes 4612
  117.9 27.2 %copy-start.5 = (f32[384]{0:T(512)S(1)}, f32[384]{0:T(512)}, u32[]{:S(2)}) copy-start(f32[384]{0:T(512)} %param.12) | copy-start | bytes 4612
  117.9 27.2 %copy-start.6 = (f32[384]{0:T(512)S(1)}, f32[384]{0:T(512)}, u32[]{:S(2)}) copy-start(f32[384]{0:T(512)} %param.14) | copy-start | bytes 4612
  117.9 99.1 %copy-start.7 = (s32[32]{0:T(128)S(1)}, s32[32]{0:T(128)}, u32[]{:S(2)}) copy-start(s32[32]{0:T(128)} %param.15) | copy-start | bytes 388
Sparse Core Ops, SparseCore 0:
  11.2 106.6 all-gather.4
